TPU v7x, 32 devices: a whole 2x2x4 slice. The times are simulated.
32 devices in a mesh: dom: 4 (over y, x), dev: 8 (over z, core).
Axes of the slice: x: 2, y: 2, z: 4, core: 2. Of those that a mesh axis runs over, the one named last changes fastest.
Arguments:
- feats: bfloat16 [65536, 256], P(('dom', 'dev')), may hold values from -6 to 6
- w_self: bfloat16 [256, 256], replicated, may hold values from -0.375 to 0.375
- w_neigh: bfloat16 [256, 256], replicated, may hold values from -0.375 to 0.375
- cotangent: bfloat16 [65536, 256], P(('dom', 'dev')), may hold values from -8 to 8
- hub_rows: int32 [1024], P(('dom', 'dev')), may hold values from 0 to 2047
- send_rows: int32 [32, 32, 16], P(('dom', 'dev')), may hold values from 0 to 2047
- send_count: int32 [32, 32], P(('dom', 'dev')), may hold values from 1 to 16, as said below
- tile_dst: int32 [10240], P(('dom', 'dev')), may hold values from 0 to 15
- tile_src: int32 [10240], P(('dom', 'dev')), may hold values from 0 to 21
- tile_count: int32 [32], P(('dom', 'dev')), may hold values from 80 to 320, as said below
- tile_val: bfloat16 [10240, 128, 128], P(('dom', 'dev')), may hold values from -0.125 to 0.125
Outputs:
- out: bfloat16 [65536, 256], P(('dom', 'dev'))
- grad_x: bfloat16 [65536, 256], P(('dom', 'dev'))
- grad_ws: float32 [256, 256], replicated
- grad_wn: float32 [256, 256], replicated
Inputs may be any that keep to these rules, and one draw needn't show every extreme that they name: `send_count`: in every draw some peer receives 16 live slots from every device. `tile_count`: each device's count is 320, 160 or 80; some device has 320.
All inputs are finite; a program needn't handle non-finite values.
Results may differ from a plain program's by a relative error of at most 0.0057.
Values may be sent and summed in bfloat16 or wider, within the bound.
No kernel may reach another device: no remote copies, remote signals or barrier semaphores. Data moves between devices by JAX's collectives and lax.ppermute only.
A program may use at most 256 MiB of HBM per device.

v0:
```python
import jax
import jax.numpy as jnp
from jax import lax
from jax.sharding import PartitionSpec as P


def tile_forward(tile_val, picked, valid):
    terms = jnp.einsum("tij,tjd->tid", tile_val, picked, preferred_element_type=jnp.float32)
    return jnp.where(valid[:, None, None], terms, jnp.float32(0.0))


def tile_backward(tile_val, spread, valid):
    terms = jnp.einsum("tij,tid->tjd", tile_val, spread, preferred_element_type=jnp.float32)
    return jnp.where(valid[:, None, None], terms, jnp.float32(0.0))


def one_hot_table(index, count, dtype):
    columns = lax.broadcasted_iota(jnp.int32, (index.shape[0], count), 1)
    return (columns == index[:, None]).astype(dtype)


def select_blocks(table, blocks):
    flat = blocks.reshape(blocks.shape[0], -1)
    chosen = jnp.dot(table, flat, preferred_element_type=jnp.float32)
    return chosen.astype(jnp.bfloat16).reshape((table.shape[0],) + blocks.shape[1:])


def add_blocks(table, terms):
    flat = terms.reshape(terms.shape[0], -1)
    contract_rows = (((0,), (0,)), ((), ()))
    summed = lax.dot_general(
        table,
        flat,
        contract_rows,
        precision=lax.Precision.HIGHEST,
        preferred_element_type=jnp.float32,
    )
    return summed


def body(
    feats,
    w_self,
    w_neigh,
    cotangent,
    hub_rows,
    send_rows,
    send_count,
    tile_dst,
    tile_src,
    tile_count,
    tile_val,
):
    edge = tile_val.shape[1]
    rows, width = feats.shape
    peers = send_rows.shape[1]
    slots = send_rows.shape[2]
    own_blocks = rows // edge
    hub_table = lax.all_gather(feats[hub_rows], "dev", axis=0, tiled=True)
    live = lax.broadcasted_iota(jnp.int32, (peers, slots), 1) < send_count[0][:, None]
    outgoing = jnp.where(live[:, :, None], feats[send_rows[0]], jnp.zeros((), jnp.bfloat16))
    incoming = lax.all_to_all(outgoing, ("dom", "dev"), split_axis=0, concat_axis=0, tiled=True)
    source = jnp.concatenate([feats, incoming.reshape(peers * slots, width), hub_table], axis=0)
    source_blocks = source.shape[0] // edge
    valid = lax.broadcasted_iota(jnp.int32, (tile_val.shape[0],), 0) < tile_count[0]
    src_table = one_hot_table(tile_src, source_blocks, jnp.bfloat16)
    dst_table = one_hot_table(tile_dst, own_blocks, jnp.bfloat16)
    dst_sums = one_hot_table(tile_dst, own_blocks, jnp.float32)
    src_sums = one_hot_table(tile_src, source_blocks, jnp.float32)
    picked = select_blocks(src_table, source.reshape(source_blocks, edge, width))
    terms = tile_forward(tile_val, picked, valid)
    agg = add_blocks(dst_sums, terms).reshape(rows, width).astype(jnp.bfloat16)
    pre = jnp.dot(feats, w_self, preferred_element_type=jnp.float32) + jnp.dot(
        agg, w_neigh, preferred_element_type=jnp.float32
    )
    sig = jax.nn.sigmoid(pre)
    out = (pre * sig).astype(jnp.bfloat16)
    dpre = (cotangent.astype(jnp.float32) * sig * (1.0 + pre * (1.0 - sig))).astype(jnp.bfloat16)
    contract_rows = (((0,), (0,)), ((), ()))
    local_ws = lax.dot_general(feats, dpre, contract_rows, preferred_element_type=jnp.float32)
    local_wn = lax.dot_general(agg, dpre, contract_rows, preferred_element_type=jnp.float32)
    summed_ws, summed_wn = lax.psum((local_ws, local_wn), ("dom", "dev"))
    scale = 1.0 / jnp.sqrt(jnp.float32(rows * peers))
    grad_ws = summed_ws * scale
    grad_wn = summed_wn * scale
    contract_cols = (((1,), (1,)), ((), ()))
    dagg = lax.dot_general(dpre, w_neigh, contract_cols, preferred_element_type=jnp.float32).astype(
        jnp.bfloat16
    )
    spread = select_blocks(dst_table, dagg.reshape(own_blocks, edge, width))
    back_terms = tile_backward(tile_val, spread, valid)
    dsource = add_blocks(src_sums, back_terms).reshape(source_blocks * edge, width)
    own = dsource[:rows]
    returning = dsource[rows : rows + peers * slots].reshape(peers, slots, width)
    hub_part = dsource[rows + peers * slots :]
    returned = lax.all_to_all(
        returning.astype(jnp.bfloat16), ("dom", "dev"), split_axis=0, concat_axis=0, tiled=True
    ).astype(returning.dtype)
    returned = jnp.where(live[:, :, None], returned, jnp.float32(0.0))
    grad = lax.dot_general(dpre, w_self, contract_cols, preferred_element_type=jnp.float32) + own
    grad = grad.at[send_rows[0].reshape(-1)].add(returned.reshape(peers * slots, width))
    hub_back = lax.psum_scatter(
        hub_part.astype(jnp.bfloat16), "dev", scatter_dimension=0, tiled=True
    ).astype(jnp.float32)
    grad = grad.at[hub_rows].add(hub_back)
    return (out, grad.astype(jnp.bfloat16), grad_ws, grad_wn)


def solution(mesh):
    return jax.shard_map(
        body,
        mesh=mesh,
        in_specs=(
            P(("dom", "dev"), None),
            P(),
            P(),
            P(("dom", "dev"), None),
            P(("dom", "dev")),
            P(("dom", "dev"), None, None),
            P(("dom", "dev"), None),
            P(("dom", "dev")),
            P(("dom", "dev")),
            P(("dom", "dev")),
            P(("dom", "dev"), None, None),
        ),
        out_specs=(P(("dom", "dev"), None), P(("dom", "dev"), None), P(), P()),
        check_vma=False,
    )
```

profile of v0, /device:TPU:0, one launch (start us, length us, event | category | flops | bytes accessed | tf_op | source)
XLA Modules:
  0.0 419.8 jit_solution(2449749782824793038)
XLA Ops:
  8.0 0.0 copy-start
  8.0 0.0 copy-start.10
  8.0 0.0 copy-start.2
  8.0 0.0 copy-start.13
  8.0 0.0 copy-start.4
  8.1 0.8 iota_compare_fusion.6
  8.9 0.7 compare_select_fusion
  9.6 0.1 copy.20
  9.7 0.1 reshape.128
  9.8 2.9 gather_fusion
  12.7 0.8 broadcast_select_fusion
  13.5 7.3 %all-to-all-start = ((bf16[32,16,256]{2,1,0:T(8,128)(2,1)}), bf16[32,16,256]{2,1,0:T(8,128)(2,1)S(1)}, u32[]{:S(2)}, u32[]{:S(2)}) async-start(bf16[32,16,256]{2,1,0:T(8,128)(2,1)} %broadcast_select_fusion), calls=%async_computation | async-start | bytes 524288 | tf_op jit(solution)/shard_map/all_to_all | solution.py:62
  20.8 0.0 all-reduce.3.cloned.1.call-start
  20.9 0.1 copy.25
  21.0 0.0 copy-start.12
  21.0 0.6 copy-done.12
  21.6 0.0 copy-done.2
  21.6 0.6 gather_fusion.1
  22.2 15.7 %all-gather = bf16[256,256]{1,0:T(8,128)(2,1)S(1)} all-gather(bf16[32,256]{1,0:T(8,128)(2,1)S(1)} %gather_fusion.1), channel_id=2, replica_groups=mesh['dom'=4,'dev'=8] {'dev'}, dimensions={0}, use_global_device_ids=true | all-gather | bytes 147456 | tf_op jit(solution)/shard_map/all_gather | solution.py:59
  38.6 0.1 reshape_squeeze.3
  38.6 0.6 compare_select_fusion.1
  39.3 1.8 fusion.8
  41.0 0.0 all-to-all-done
  41.0 1.2 pad_maximum_fusion
  42.2 2.5 reshape_reshape.6
  44.8 10.0 %convolution_convert_fusion.1 = bf16[320,32768]{1,0:T(8,128)(2,1)} fusion(bf16[22,32768]{1,0:T(8,128)(2,1)S(1)} %reshape_reshape.6, s32[320]{0:T(512)S(1)} %copy-done.5), kind=kOutput, calls=%fused_computation.5 | convolution fusion | flops 471866240 | bytes 22414592 | tf_op jit(solution)/shard_map/dot_general | solution.py:24
  54.8 19.3 %copy.32 = bf16[40,8,128,256]{3,2,1,0:T(8,128)(2,1)} copy(bf16[40,8,128,256]{3,1,2,0:T(8,128)(2,1)} %bitcast.53) | data formatting | bytes 41943040
  74.1 31.5 %select_bitcast_fusion.1 = f32[320,128,256]{1,2,0:T(8,128)} fusion(pred[320]{0:T(512)(128)(4,1)S(1)} %iota_compare_fusion.7, bf16[320,128,256]{2,1,0:T(8,128)(2,1)} %bitcast.52, bf16[320,128,128]{2,1,0:T(8,128)(2,1)} %param.21), kind=kOutput, calls=%fused_computation.7 | convolution fusion | flops 2694840320 | bytes 73400640 | tf_op jit(solution)/shard_map/tij,tjd->tid/dot_general | solution.py:8
  105.6 41.9 %copy.33 = f32[40,8,128,256]{3,1,2,0:T(8,128)} copy(f32[40,8,128,256]{2,3,1,0:T(8,128)} %bitcast.48) | data formatting | bytes 83886080
  147.6 0.0 copy-done.7
  147.6 18.6 %convolution_convert_fusion.2 = bf16[16,32768]{1,0:T(8,128)(2,1)S(1)} fusion(f32[320,32768]{1,0:T(8,128)} %bitcast.50, s32[320]{0:T(512)S(1)} %copy-done.7), kind=kOutput, calls=%fused_computation.8 | convolution fusion | flops 2013795328 | bytes 42992896 | tf_op jit(solution)/shard_map/dot_general | solution.py:31
  166.2 1.3 convert_element_type.47
  167.5 4.5 %multiply_convert_fusion = (bf16[2048,256]{1,0:T(8,128)(2,1)S(1)}, bf16[2048,256]{1,0:T(8,128)(2,1)}) fusion(bf16[2048,256]{1,0:T(8,128)(2,1)} %param.14, f32[2048,256]{1,0:T(8,128)} %fusion.8, bf16[2048,256]{1,0:T(8,128)(2,1)} %convert_element_type.47, bf16[256,256]{1,0:T(8,128)(2,1)S(1)} %copy-done), kind=kOutput, calls=%fused_computation.12 | convolution fusion | flops 275251200 | bytes 6422528 | tf_op jit(solution)/shard_map/dot_general | solution.py:73
  172.0 1.2 fusion.9
  173.2 1.2 convolution_bitcast_fusion
  174.4 0.5 convolution_convert_fusion.3
  174.9 0.5 reshape_reshape.7
  175.4 9.9 %convolution_convert_fusion = bf16[320,32768]{1,0:T(8,128)(2,1)} fusion(bf16[16,32768]{1,0:T(8,128)(2,1)S(1)} %reshape_reshape.7, s32[320]{0:T(512)S(1)} %copy-done.7), kind=kOutput, calls=%fused_computation.4 | convolution fusion | flops 346035200 | bytes 22021376 | tf_op jit(solution)/shard_map/dot_general | solution.py:24
  185.3 19.4 %copy.34 = bf16[40,8,128,256]{3,2,1,0:T(8,128)(2,1)} copy(bf16[40,8,128,256]{3,1,2,0:T(8,128)(2,1)} %bitcast.54) | data formatting | bytes 41943040
  204.7 27.8 %select_bitcast_fusion = f32[320,128,256]{1,2,0:T(8,128)} fusion(pred[320]{0:T(512)(128)(4,1)S(1)} %iota_compare_fusion.7, bf16[320,128,256]{2,1,0:T(8,128)(2,1)} %bitcast.51, bf16[320,128,128]{2,1,0:T(8,128)(2,1)} %param.21), kind=kOutput, calls=%fused_computation.6 | convolution fusion | flops 2694840320 | bytes 73400640 | tf_op jit(solution)/shard_map/tij,tid->tjd/dot_general | solution.py:13
  232.5 42.0 %copy.35 = f32[40,8,128,256]{3,1,2,0:T(8,128)} copy(f32[40,8,128,256]{2,3,1,0:T(8,128)} %bitcast.47) | data formatting | bytes 83886080
  274.5 0.0 all-reduce.3.cloned.1.call-update
  274.5 19.1 %fusion.7 = (bf16[22,32768]{1,0:T(8,128)(2,1)S(1)}, f32[22,32768]{1,0:T(8,128)S(1)}) fusion(f32[320,32768]{1,0:T(8,128)} %bitcast.49, s32[320]{0:T(512)S(1)} %copy-done.6), kind=kOutput, calls=%fused_computation.37 | convolution fusion | flops 2768968704 | bytes 46269696 | tf_op jit(solution)/shard_map/dot_general | solution.py:31
  293.6 0.1 slice.25
  293.7 0.1 slice.26
  293.9 0.1 slice.24
  294.0 1.5 slice.17
  295.5 0.9 convert_element_type.53
  296.4 4.2 all-to-all-start.1
  300.6 0.0 reduce-scatter.2.cloned.1.call-start
  300.6 0.7 convert_element_type.55
  301.4 0.0 reduce-scatter.2.cloned.1.call-update
  301.4 2.1 convolution_add_fusion
  303.6 98.9 %all-reduce.3.cloned.1.call-done = (f32[256,256]{0,1:T(8,128)}, f32[256,256]{0,1:T(8,128)}) async-done(((f32[256,256]{0,1:T(8,128)}, f32[256,256]{0,1:T(8,128)}), (f32[256,256]{0,1:T(8,128)}, f32[256,256]{0,1:T(8,128)})) %all-reduce.3.cloned.1.call-update) | async-done | bytes 524304 | tf_op jit(solution)/shard_map/psum | solution.py:82
  402.4 1.1 broadcast_multiply_fusion
  403.5 0.8 copy.27
  404.4 0.8 copy.28
  405.2 0.0 all-to-all-done.1
  405.2 0.1 convert_select_fusion
  405.3 0.0 copy-start.1
  405.4 4.1 scatter_fusion
  409.5 0.0 reduce-scatter.2.cloned.1.call-done
  409.5 1.7 scatter_custom_fusion.1
  411.2 1.1 convert_element_type.57
  (22 shorter events, 0.1 us)
Async XLA Ops:
  8.0 159.5 %copy-start = (bf16[256,256]{1,0:T(8,128)(2,1)S(1)}, bf16[256,256]{1,0:T(8,128)(2,1)}, u32[]{:S(2)}) copy-start(bf16[256,256]{1,0:T(8,128)(2,1)} %param.13) | copy-start | bytes 393220
  8.0 12.9 %copy-start.10 = (s32[1,32,16]{1,2,0:T(8,128)S(1)}, s32[1,32,16]{1,2,0:T(8,128)}, u32[]{:S(2)}) copy-start(s32[1,32,16]{1,2,0:T(8,128)} %param.16) | copy-start | bytes 6148
  8.0 13.6 %copy-start.2 = (bf16[2048,256]{1,0:T(8,128)(2,1)S(1)}, bf16[2048,256]{1,0:T(8,128)(2,1)}, u32[]{:S(2)}) copy-start(bf16[2048,256]{1,0:T(8,128)(2,1)} %param.11) | copy-start | bytes 3145732
  8.0 12.9 %copy-start.13 = (s32[32]{0:T(128)S(1)}, s32[32]{0:T(128)}, u32[]{:S(2)}) copy-start(s32[32]{0:T(128)} %param.15) | copy-start | bytes 388
  8.0 31.2 %copy-start.4 = (bf16[256,256]{1,0:T(8,128)(2,1)S(1)}, bf16[256,256]{1,0:T(8,128)(2,1)}, u32[]{:S(2)}) copy-start(bf16[256,256]{1,0:T(8,128)(2,1)} %param.12) | copy-start | bytes 393220
  8.9 12.7 %copy-start.8 = (pred[32,16]{1,0:T(8,128)(4,1)}, pred[32,16]{1,0:T(8,128)(4,1)S(1)}, u32[]{:S(2)}) copy-start(pred[32,16]{1,0:T(8,128)(4,1)S(1)} %iota_compare_fusion.6) | copy-start | bytes 1540
  13.5 27.5 %all-to-all-start = ((bf16[32,16,256]{2,1,0:T(8,128)(2,1)}), bf16[32,16,256]{2,1,0:T(8,128)(2,1)S(1)}, u32[]{:S(2)}, u32[]{:S(2)}) async-start(bf16[32,16,256]{2,1,0:T(8,128)(2,1)} %broadcast_select_fusion), calls=%async_computation | async-start | bytes 524288 | tf_op jit(solution)/shard_map/all_to_all | solution.py:62
  20.8 381.6 %all-reduce.3.cloned.1.call-start = ((), (), s32[]{:S(2)}) async-start(), calls=%async_computation.4 | async-start | bytes 1048576 | tf_op jit(solution)/shard_map/psum | solution.py:82
  21.0 0.6 copy-start.12
  41.0 3.8 copy-start.5
  105.6 41.9 %copy-start.7 = (s32[320]{0:T(512)S(1)}, s32[320]{0:T(512)}, u32[]{:S(2)}) copy-start(s32[320]{0:T(512)} %param.18) | copy-start | bytes 3844
  167.5 4.5 %copy-start.3 = (bf16[2048,256]{1,0:T(8,128)(2,1)S(1)}, bf16[2048,256]{1,0:T(8,128)(2,1)}, u32[]{:S(2)}) copy-start(bf16[2048,256]{1,0:T(8,128)(2,1)} %convert_element_type.47) | copy-start | bytes 3145732
  232.5 42.0 %copy-start.6 = (s32[320]{0:T(512)S(1)}, s32[320]{0:T(512)}, u32[]{:S(2)}) copy-start(s32[320]{0:T(512)} %param.19) | copy-start | bytes 3844
  296.4 108.8 %all-to-all-start.1 = ((bf16[32,16,256]{2,1,0:T(8,128)(2,1)}), bf16[32,16,256]{2,1,0:T(8,128)(2,1)S(1)}, u32[]{:S(2)}, u32[]{:S(2)}) async-start(bf16[32,16,256]{2,1,0:T(8,128)(2,1)} %convert_element_type.53), calls=%async_computation.1 | async-start | bytes 524288 | tf_op jit(solution)/shard_map/all_to_all | solution.py:96
  300.6 108.9 %reduce-scatter.2.cloned.1.call-start = ((), (), s32[]{:S(2)}) async-start(), calls=%async_computation.3 | async-start | bytes 147456 | tf_op jit(solution)/shard_map/reduce_scatter | solution.py:102
  301.4 103.8 %copy-start.9 = (pred[32,16]{1,0:T(8,128)(4,1)S(1)}, pred[32,16]{1,0:T(8,128)(4,1)}, u32[]{:S(2)}) copy-start(pred[32,16]{1,0:T(8,128)(4,1)} %copy-done.8) | copy-start | bytes 1540
  301.4 103.9 %copy-start.11 = (s32[512,1]{0,1:T(1,128)S(1)}, s32[512,1]{0,1:T(1,128)}, u32[]{:S(2)}) copy-start(s32[512,1]{0,1:T(1,128)} %compare_select_fusion.1) | copy-start | bytes 6148
  405.3 7.0 %copy-start.1 = (bf16[256,256]{1,0:T(8,128)(2,1)S(1)}, bf16[256,256]{1,0:T(8,128)(2,1)}, u32[]{:S(2)}) copy-start(bf16[256,256]{1,0:T(8,128)(2,1)} %param.13) | copy-start | bytes 393220
Sparse Core Ops, SparseCore 0:
  274.6 127.7 all-reduce.2
Sparse Core Ops, SparseCore 1:
  303.3 31.4 reduce-scatter.1
where the time goes:
time: 422 us; the launch traced here: 420 us
  local copies, waits for them, and re-layouts  137 us (32%)
  matrix products  128 us (30%)
  waiting for transfers between devices  99 us (23%)
  between operations  16.4 us (4%)
  blocking collectives  15.7 us (4%)
  other arithmetic  12.3 us (3%)
  starting transfers between devices  11.5 us (3%)
    unnamed x35, local copies, waits for them, and re-layouts  125 us
    psum x1, waiting for transfers between devices, body(): summed_ws, summed_wn = lax.psum((local_ws, local_wn), ('dom', 'dev'))  98.9 us
    dot_general x2, matrix products, add_blocks(): lax.dot_general(table, flat, contract_rows, precision=lax.Precision.HIGHE...  37.8 us
    dot_general x1, matrix products, tile_forward(): jnp.einsum('tij,tjd->tid', tile_val, picked, preferred_element_type=jnp.f...  31.5 us
    dot_general x1, matrix products, tile_backward(): jnp.einsum('tij,tid->tjd', tile_val, spread, preferred_element_type=jnp.f...  27.8 us
    dot_general x2, matrix products, select_blocks(): chosen = jnp.dot(table, flat, preferred_element_type=jnp.float32)  19.9 us
    all_gather x1, blocking collectives, body(): hub_table = lax.all_gather(feats[hub_rows], 'dev', axis=0, tiled=True)  15.7 us
  transfers between devices with their start and end apart: 4, of which 1 were waited for; matrix products, arithmetic and copies ran while one was open for 8% of the time, Pallas kernels for 0%

commit v1 on v0

--- a/solution.py
+++ b/solution.py
@@ -2,6 +2,12 @@
 import jax.numpy as jnp
 from jax import lax
 from jax.sharding import PartitionSpec as P
+
+
+def in_order(blocks, dim):
+    dims = list(blocks.shape[1:])
+    dims[dim] *= blocks.shape[0]
+    return jnp.moveaxis(blocks, 0, dim).reshape(dims)
 
 
 def tile_forward(tile_val, picked, valid):
@@ -56,7 +62,19 @@
     peers = send_rows.shape[1]
     slots = send_rows.shape[2]
     own_blocks = rows // edge
-    hub_table = lax.all_gather(feats[hub_rows], "dev", axis=0, tiled=True)
+    size = lax.axis_size("dev")
+    pairs = [(i, (i + 1) % size) for i in range(size)]
+    back = [(b, a) for a, b in pairs]
+    lower, upper = ([], [])
+    for lap in range(size - 1):
+        if lap % 2 == 0:
+            lower.append(lax.ppermute(lower[-1] if lower else feats[hub_rows], "dev", pairs))
+        else:
+            upper.append(lax.ppermute(upper[-1] if upper else feats[hub_rows], "dev", back))
+    tiles = jnp.stack([*lower[::-1], feats[hub_rows], *upper])
+    shift = lax.axis_index("dev") - len(lower)
+    tiles = tiles[(jnp.arange(size) - shift) % size]
+    hub_table = in_order(tiles, 0)
     live = lax.broadcasted_iota(jnp.int32, (peers, slots), 1) < send_count[0][:, None]
     outgoing = jnp.where(live[:, :, None], feats[send_rows[0]], jnp.zeros((), jnp.bfloat16))
     incoming = lax.all_to_all(outgoing, ("dom", "dev"), split_axis=0, concat_axis=0, tiled=True)

time: 422 us -> 467 us (1.11)
  waiting for transfers between devices: 99 us -> 142 us
  blocking collectives: 15.7 us -> 0 us
  starting transfers between devices: 11.5 us -> 22.3 us
    psum x1, waiting for transfers between devices: 98.9 us -> 132 us  [body(): summed_ws, summed_wn = lax.psum((local_ws, local_wn), ('dom', 'dev'))]
    all_gather x1 -> x0, blocking collectives: 15.7 us -> none  [body(): hub_table = lax.all_gather(feats[hub_rows], 'dev', axis=0, tiled=True)]
    ppermute x0 -> x7, starting transfers between devices: none -> 12 us  [the longest x3 11.2 us: body(): lax.ppermute(upper[-1] if upper else feats[hub_rows], 'dev', back)]
    ppermute x0 -> x7, waiting for transfers between devices: none -> 8.83 us  [the longest x4 7.53 us: body(): lax.ppermute(lower[-1] if lower else feats[hub_rows], 'dev', pairs)]
    unnamed x35 -> x42, local copies, waits for them, and re-layouts: 125 us -> 124 us
  transfers between devices with their start and end apart: 4 -> 11, of which waited for: 1 -> 6; matrix products, arithmetic and copies ran while one was open for 8% -> 4% of each run, Pallas kernels for 0% -> 0%
where the time goes in v1:
time: 467 us; the launch traced here: 464 us
  waiting for transfers between devices  142 us (30%)
  local copies, waits for them, and re-layouts  140 us (30%)
  matrix products  130 us (28%)
  starting transfers between devices  22.3 us (5%)
  between operations  16.4 us (4%)
  other arithmetic  13.8 us (3%)
    psum x1, waiting for transfers between devices, body(): summed_ws, summed_wn = lax.psum((local_ws, local_wn), ('dom', 'dev'))  132 us
    unnamed x42, local copies, waits for them, and re-layouts  124 us
    dot_general x2, matrix products, add_blocks(): lax.dot_general(table, flat, contract_rows, precision=lax.Precision.HIGHE...  39.2 us
    dot_general x1, matrix products, tile_forward(): jnp.einsum('tij,tjd->tid', tile_val, picked, preferred_element_type=jnp.f...  31.6 us
    dot_general x1, matrix products, tile_backward(): jnp.einsum('tij,tid->tjd', tile_val, spread, preferred_element_type=jnp.f...  27.9 us
    dot_general x2, matrix products, select_blocks(): chosen = jnp.dot(table, flat, preferred_element_type=jnp.float32)  19.9 us
    ppermute x3, starting transfers between devices, body(): lax.ppermute(upper[-1] if upper else feats[hub_rows], 'dev', back)  11.2 us
  transfers between devices with their start and end apart: 11, of which 6 were waited for; matrix products, arithmetic and copies ran while one was open for 4% of the time, Pallas kernels for 0%

profile of v1, /device:TPU:0, one launch (start us, length us, event | category | flops | bytes accessed | tf_op | source)
XLA Modules:
  0.0 464.3 jit_solution(15761482599136234276)
XLA Ops:
  8.1 0.8 compare_select_fusion.3
  8.8 0.7 compare_select_fusion
  9.5 0.1 copy.20
  9.6 0.1 reshape.181
  9.7 2.0 gather_fusion.1
  11.6 0.5 collective-permute-start
  12.2 4.1 collective-permute-start.4
  16.3 2.9 gather_fusion
  19.2 0.7 iota_compare_fusion.6
  19.9 0.8 broadcast_select_fusion
  20.8 4.5 all-to-all-start
  25.3 0.1 copy.25
  25.4 1.8 fusion.10
  27.1 0.1 reshape_squeeze.3
  27.2 0.6 compare_select_fusion.1
  27.8 0.2 collective-permute-start.1
  28.1 6.0 %collective-permute-done.1 = bf16[32,256]{1,0:T(8,128)(2,1)S(1)} collective-permute-done((bf16[32,256]{1,0:T(8,128)(2,1)S(1)}, bf16[32,256]{1,0:T(8,128)(2,1)S(1)}, u32[]{:S(2)}, u32[]{:S(2)}) %collective-permute-start.1) | collective-permute-done | bytes 16416 | tf_op jit(solution)/shard_map/ppermute | solution.py:71
  34.7 3.6 collective-permute-start.5
  38.3 0.8 collective-permute-done.2
  39.1 0.7 collective-permute-done.5
  39.8 3.5 collective-permute-start.6
  43.3 0.8 collective-permute-done.3
  44.1 0.6 collective-permute-done.6
  44.7 0.6 gather_fusion.2
  45.3 1.2 pad_maximum_fusion
  46.6 2.5 reshape_reshape.6
  49.1 10.0 %convolution_convert_fusion.1 = bf16[320,32768]{1,0:T(8,128)(2,1)} fusion(bf16[22,32768]{1,0:T(8,128)(2,1)S(1)} %reshape_reshape.6, s32[320]{0:T(512)S(1)} %copy-done.6), kind=kOutput, calls=%fused_computation.6 | convolution fusion | flops 471866240 | bytes 22414592 | tf_op jit(solution)/shard_map/dot_general | solution.py:30
  59.1 19.4 %copy.32 = bf16[40,8,128,256]{3,2,1,0:T(8,128)(2,1)} copy(bf16[40,8,128,256]{3,1,2,0:T(8,128)(2,1)} %bitcast.72) | data formatting | bytes 41943040
  78.4 31.6 %select_bitcast_fusion.1 = f32[320,128,256]{1,2,0:T(8,128)} fusion(pred[320]{0:T(512)(128)(4,1)S(1)} %iota_compare_fusion.7, bf16[320,128,256]{2,1,0:T(8,128)(2,1)} %bitcast.71, bf16[320,128,128]{2,1,0:T(8,128)(2,1)} %param.21), kind=kOutput, calls=%fused_computation.8 | convolution fusion | flops 2694840320 | bytes 73400640 | tf_op jit(solution)/shard_map/tij,tjd->tid/dot_general | solution.py:14
  110.0 42.0 %copy.33 = f32[40,8,128,256]{3,1,2,0:T(8,128)} copy(f32[40,8,128,256]{2,3,1,0:T(8,128)} %bitcast.67) | data formatting | bytes 83886080
  152.0 18.6 %convolution_convert_fusion.2 = bf16[16,32768]{1,0:T(8,128)(2,1)S(1)} fusion(f32[320,32768]{1,0:T(8,128)} %bitcast.69, s32[320]{0:T(512)S(1)} %copy-done.8), kind=kOutput, calls=%fused_computation.9 | convolution fusion | flops 2013795328 | bytes 42992896 | tf_op jit(solution)/shard_map/dot_general | solution.py:37
  170.6 1.3 convert_element_type.47
  172.0 4.5 multiply_convert_fusion
  176.5 1.2 fusion.11
  177.7 1.2 convolution_bitcast_fusion
  178.9 0.5 convolution_convert_fusion.3
  179.3 0.5 reshape_reshape.7
  179.9 10.0 %convolution_convert_fusion = bf16[320,32768]{1,0:T(8,128)(2,1)} fusion(bf16[16,32768]{1,0:T(8,128)(2,1)S(1)} %reshape_reshape.7, s32[320]{0:T(512)S(1)} %copy-done.8), kind=kOutput, calls=%fused_computation.5 | convolution fusion | flops 346035200 | bytes 22021376 | tf_op jit(solution)/shard_map/dot_general | solution.py:30
  189.8 19.4 %copy.34 = bf16[40,8,128,256]{3,2,1,0:T(8,128)(2,1)} copy(bf16[40,8,128,256]{3,1,2,0:T(8,128)(2,1)} %bitcast.73) | data formatting | bytes 41943040
  209.2 27.9 %select_bitcast_fusion = f32[320,128,256]{1,2,0:T(8,128)} fusion(pred[320]{0:T(512)(128)(4,1)S(1)} %iota_compare_fusion.7, bf16[320,128,256]{2,1,0:T(8,128)(2,1)} %bitcast.70, bf16[320,128,128]{2,1,0:T(8,128)(2,1)} %param.21), kind=kOutput, calls=%fused_computation.7 | convolution fusion | flops 2694840320 | bytes 73400640 | tf_op jit(solution)/shard_map/tij,tid->tjd/dot_general | solution.py:19
  237.0 42.0 %copy.35 = f32[40,8,128,256]{3,1,2,0:T(8,128)} copy(f32[40,8,128,256]{2,3,1,0:T(8,128)} %bitcast.66) | data formatting | bytes 83886080
  279.0 20.6 %fusion.9 = (bf16[22,32768]{1,0:T(8,128)(2,1)}, f32[22,32768]{1,0:T(8,128)S(1)}) fusion(f32[320,32768]{1,0:T(8,128)} %bitcast.68, s32[320]{0:T(512)S(1)} %copy-done.7), kind=kOutput, calls=%fused_computation.53 | convolution fusion | flops 2768968704 | bytes 46269696 | tf_op jit(solution)/shard_map/dot_general | solution.py:37
  299.6 0.1 slice.26
  299.7 1.5 slice.17
  301.2 1.1 slice.27
  302.3 0.9 convert_element_type.53
  303.2 5.7 %all-to-all-start.1 = ((bf16[32,16,256]{2,1,0:T(8,128)(2,1)}), bf16[32,16,256]{2,1,0:T(8,128)(2,1)S(1)}, u32[]{:S(2)}, u32[]{:S(2)}) async-start(bf16[32,16,256]{2,1,0:T(8,128)(2,1)} %convert_element_type.53), calls=%async_computation.1 | async-start | bytes 524288 | tf_op jit(solution)/shard_map/all_to_all | solution.py:114
  309.0 0.0 all-reduce.3.cloned.1.call-start
  309.0 0.7 all-reduce.3.cloned.1.call-update
  309.7 0.0 reduce-scatter.2.cloned.1.call-start
  309.8 2.1 convolution_add_fusion
  311.8 1.2 slice.28
  313.0 0.7 convert_element_type.55
  313.7 0.0 reduce-scatter.2.cloned.1.call-update
  313.8 132.4 %all-reduce.3.cloned.1.call-done = (f32[256,256]{0,1:T(8,128)}, f32[256,256]{0,1:T(8,128)}) async-done(((f32[256,256]{0,1:T(8,128)}, f32[256,256]{0,1:T(8,128)}), (f32[256,256]{0,1:T(8,128)}, f32[256,256]{0,1:T(8,128)})) %all-reduce.3.cloned.1.call-update) | async-done | bytes 524304 | tf_op jit(solution)/shard_map/psum | solution.py:100
  446.1 1.0 broadcast_multiply_fusion.1
  447.1 1.0 broadcast_multiply_fusion
  448.1 0.8 copy.27
  448.9 0.8 copy.28
  449.8 0.1 convert_select_fusion
  449.9 4.1 scatter_fusion
  454.0 0.0 reduce-scatter.2.cloned.1.call-done
  454.1 1.7 scatter_custom_fusion.1
  455.8 1.1 convert_element_type.57
  (46 shorter events, 0.1 us)
Async XLA Ops:
  8.0 164.0 %copy-start = (bf16[256,256]{1,0:T(8,128)(2,1)S(1)}, bf16[256,256]{1,0:T(8,128)(2,1)}, u32[]{:S(2)}) copy-start(bf16[256,256]{1,0:T(8,128)(2,1)} %param.13) | copy-start | bytes 393220
  8.0 17.3 %copy-start.11 = (s32[1,32,16]{1,2,0:T(8,128)S(1)}, s32[1,32,16]{1,2,0:T(8,128)}, u32[]{:S(2)}) copy-start(s32[1,32,16]{1,2,0:T(8,128)} %param.16) | copy-start | bytes 6148
  8.0 17.3 %copy-start.2 = (bf16[2048,256]{1,0:T(8,128)(2,1)S(1)}, bf16[2048,256]{1,0:T(8,128)(2,1)}, u32[]{:S(2)}) copy-start(bf16[2048,256]{1,0:T(8,128)(2,1)} %param.11) | copy-start | bytes 3145732
  8.0 17.3 %copy-start.4 = (bf16[256,256]{1,0:T(8,128)(2,1)S(1)}, bf16[256,256]{1,0:T(8,128)(2,1)}, u32[]{:S(2)}) copy-start(bf16[256,256]{1,0:T(8,128)(2,1)} %param.12) | copy-start | bytes 393220
  8.8 12.0 %copy-start.13 = (s32[32]{0:T(128)}, s32[32]{0:T(128)S(1)}, u32[]{:S(2)}) copy-start(s32[32]{0:T(128)S(1)} %compare_select_fusion.3) | copy-start | bytes 388
  11.6 16.1 %collective-permute-start = (bf16[32,256]{1,0:T(8,128)(2,1)S(1)}, bf16[32,256]{1,0:T(8,128)(2,1)S(1)}, u32[]{:S(2)}, u32[]{:S(2)}) collective-permute-start(bf16[32,256]{1,0:T(8,128)(2,1)S(1)} %gather_fusion.1), channel_id=1, source_target_pairs={{0,1},{1,2},{2,3},{3,4},{4,5},{5,6},{6,7},{7,0},{8,9},{9,10},{10,1... | collective-permute-start | bytes 49160 | tf_op jit(solution)/shard_map/ppermute | solution.py:71
  12.2 22.6 %collective-permute-start.4 = (bf16[32,256]{1,0:T(8,128)(2,1)S(1)}, bf16[32,256]{1,0:T(8,128)(2,1)S(1)}, u32[]{:S(2)}, u32[]{:S(2)}) collective-permute-start(bf16[32,256]{1,0:T(8,128)(2,1)S(1)} %gather_fusion.1), channel_id=1, source_target_pairs={{1,0},{2,1},{3,2},{4,3},{5,4},{6,5},{7,6},{0,7},{9,8},{10,9},{11,1... | collective-permute-start | bytes 49160 | tf_op jit(solution)/shard_map/ppermute | solution.py:73
  19.9 0.8 copy-start.9
  20.8 24.5 %all-to-all-start = ((bf16[32,16,256]{2,1,0:T(8,128)(2,1)}), bf16[32,16,256]{2,1,0:T(8,128)(2,1)S(1)}, u32[]{:S(2)}, u32[]{:S(2)}) async-start(bf16[32,16,256]{2,1,0:T(8,128)(2,1)} %broadcast_select_fusion), calls=%async_computation | async-start | bytes 524288 | tf_op jit(solution)/shard_map/all_to_all | solution.py:80
  27.8 6.3 %collective-permute-start.1 = (bf16[32,256]{1,0:T(8,128)(2,1)S(1)}, bf16[32,256]{1,0:T(8,128)(2,1)S(1)}, u32[]{:S(2)}, u32[]{:S(2)}) collective-permute-start(bf16[32,256]{1,0:T(8,128)(2,1)S(1)} %collective-permute-done), channel_id=1, source_target_pairs={{0,1},{1,2},{2,3},{3,4},{4,5},{5,6},{6,7},{7,0},{8,9},{9,10},{10,1... | collective-permute-start | bytes 49160 | tf_op jit(solution)/shard_map/ppermute | solution.py:71
  34.1 5.0 %collective-permute-start.2 = (bf16[32,256]{1,0:T(8,128)(2,1)S(1)}, bf16[32,256]{1,0:T(8,128)(2,1)S(1)}, u32[]{:S(2)}, u32[]{:S(2)}) collective-permute-start(bf16[32,256]{1,0:T(8,128)(2,1)S(1)} %collective-permute-done.1), channel_id=1, source_target_pairs={{0,1},{1,2},{2,3},{3,4},{4,5},{5,6},{6,7},{7,0},{8,9},{9,10},{10,1... | collective-permute-start | bytes 49160 | tf_op jit(solution)/shard_map/ppermute | solution.py:71
  34.7 5.0 %collective-permute-start.5 = (bf16[32,256]{1,0:T(8,128)(2,1)S(1)}, bf16[32,256]{1,0:T(8,128)(2,1)S(1)}, u32[]{:S(2)}, u32[]{:S(2)}) collective-permute-start(bf16[32,256]{1,0:T(8,128)(2,1)S(1)} %collective-permute-done.4), channel_id=1, source_target_pairs={{1,0},{2,1},{3,2},{4,3},{5,4},{6,5},{7,6},{0,7},{9,8},{10,9},{11,1... | collective-permute-start | bytes 49160 | tf_op jit(solution)/shard_map/ppermute | solution.py:73
  39.1 5.0 %collective-permute-start.3 = (bf16[32,256]{1,0:T(8,128)(2,1)S(1)}, bf16[32,256]{1,0:T(8,128)(2,1)S(1)}, u32[]{:S(2)}, u32[]{:S(2)}) collective-permute-start(bf16[32,256]{1,0:T(8,128)(2,1)S(1)} %collective-permute-done.2), channel_id=1, source_target_pairs={{0,1},{1,2},{2,3},{3,4},{4,5},{5,6},{6,7},{7,0},{8,9},{9,10},{10,1... | collective-permute-start | bytes 49160 | tf_op jit(solution)/shard_map/ppermute | solution.py:71
  39.8 5.0 %collective-permute-start.6 = (bf16[32,256]{1,0:T(8,128)(2,1)S(1)}, bf16[32,256]{1,0:T(8,128)(2,1)S(1)}, u32[]{:S(2)}, u32[]{:S(2)}) collective-permute-start(bf16[32,256]{1,0:T(8,128)(2,1)S(1)} %collective-permute-done.5), channel_id=1, source_target_pairs={{1,0},{2,1},{3,2},{4,3},{5,4},{6,5},{7,6},{0,7},{9,8},{10,9},{11,1... | collective-permute-start | bytes 49160 | tf_op jit(solution)/shard_map/ppermute | solution.py:73
  45.3 3.8 copy-start.6
  110.0 42.0 %copy-start.8 = (s32[320]{0:T(512)S(1)}, s32[320]{0:T(512)}, u32[]{:S(2)}) copy-start(s32[320]{0:T(512)} %param.18) | copy-start | bytes 3844
  172.0 4.5 copy-start.3
  237.0 42.0 %copy-start.7 = (s32[320]{0:T(512)S(1)}, s32[320]{0:T(512)}, u32[]{:S(2)}) copy-start(s32[320]{0:T(512)} %param.19) | copy-start | bytes 3844
  299.7 10.1 %copy-start.5 = (bf16[256,256]{1,0:T(8,128)(2,1)S(1)}, bf16[256,256]{1,0:T(8,128)(2,1)}, u32[]{:S(2)}) copy-start(bf16[256,256]{1,0:T(8,128)(2,1)} %param.12) | copy-start | bytes 393220
  303.2 146.6 %all-to-all-start.1 = ((bf16[32,16,256]{2,1,0:T(8,128)(2,1)}), bf16[32,16,256]{2,1,0:T(8,128)(2,1)S(1)}, u32[]{:S(2)}, u32[]{:S(2)}) async-start(bf16[32,16,256]{2,1,0:T(8,128)(2,1)} %convert_element_type.53), calls=%async_computation.1 | async-start | bytes 524288 | tf_op jit(solution)/shard_map/all_to_all | solution.py:114
  309.0 137.2 %all-reduce.3.cloned.1.call-start = ((), (), s32[]{:S(2)}) async-start(), calls=%async_computation.4 | async-start | bytes 1048576 | tf_op jit(solution)/shard_map/psum | solution.py:100
  309.7 140.1 %copy-start.10 = (pred[32,16]{1,0:T(8,128)(4,1)S(1)}, pred[32,16]{1,0:T(8,128)(4,1)}, u32[]{:S(2)}) copy-start(pred[32,16]{1,0:T(8,128)(4,1)} %copy-done.9) | copy-start | bytes 1540
  309.7 144.4 %reduce-scatter.2.cloned.1.call-start = ((), (), s32[]{:S(2)}) async-start(), calls=%async_computation.3 | async-start | bytes 147456 | tf_op jit(solution)/shard_map/reduce_scatter | solution.py:120
  311.8 138.1 %copy-start.12 = (s32[512,1]{0,1:T(1,128)S(1)}, s32[512,1]{0,1:T(1,128)}, u32[]{:S(2)}) copy-start(s32[512,1]{0,1:T(1,128)} %compare_select_fusion.1) | copy-start | bytes 6148
  449.9 7.0 %copy-start.1 = (bf16[256,256]{1,0:T(8,128)(2,1)S(1)}, bf16[256,256]{1,0:T(8,128)(2,1)}, u32[]{:S(2)}) copy-start(bf16[256,256]{1,0:T(8,128)(2,1)} %param.13) | copy-start | bytes 393220
Sparse Core Ops, SparseCore 0:
  316.7 129.3 all-reduce.2
Sparse Core Ops, SparseCore 1:
  313.9 31.3 reduce-scatter.1
